TPU v7x, 256 devices: a whole 4x4x8 slice. The times are simulated.
256 devices in a mesh: seq: 16 (over y, x), fsdp: 16 (over z, core).
Axes of the slice: x: 4, y: 4, z: 8, core: 2. Of those that a mesh axis runs over, the one named last changes fastest.
Arguments:
- byte_rows: bfloat16 [16, 16384, 512], P('fsdp', 'seq'), may hold values from -6 to 6
- cotangent: bfloat16 [16, 16384, 512], P('fsdp', 'seq'), may hold values from -6 to 6
- doc_ids: int32 [16, 16384], P('fsdp', 'seq'), may hold values from 0 to 31, never falling along the last dimension, each value on 1 to 2048 neighbouring positions
- conv_weight: bfloat16 [8, 32, 16, 16], replicated, may hold values from -0.5 to 0.5
- norm_gain: float32 [512], replicated, may hold values from 0.5 to 1.5
- proj_weight: bfloat16 [4096, 512], P('fsdp'), may hold values from -0.25 to 0.25
- round_seed: int32 [1], replicated, may hold values from 0 to 1073741823
- step_count: int32 [1], replicated, may hold values from 0 to 999999
Outputs:
- grad_bytes: float32 [16, 16384, 512], P('fsdp', 'seq')
- grad_proj: float32 [4096, 512], P('fsdp')
- grad_conv: float32 [8, 32, 16, 16], replicated
- grad_gain: float32 [512], replicated
Inputs may be any that keep to these rules, and one draw needn't show every extreme that they name: `doc_ids`: along each sequence the document numbers never fall; no document covers more than 2048 bytes, and one covers exactly 2048.
All inputs are finite; a program needn't handle non-finite values.
Results may differ from a plain program's by a relative error of at most 0.0046.
Values may be sent and summed in bfloat16 or wider, within the bound.
No kernel may reach another device: no remote copies, remote signals or barrier semaphores. Data moves between devices by JAX's collectives and lax.ppermute only.
A program may use at most 128 MiB of HBM per device.

v0:
```python
import math
import jax
import jax.numpy as jnp
from jax import lax
from jax.sharding import PartitionSpec as P

GROUPS = 32
KERNEL = 8
STRIDE = 4
CG = 16
GELU_A = 0.7978845608028654
GELU_B = 0.044715
QUANT = 0.25


def shifted(value, axis, steps):
    count = lax.axis_size(axis)
    initial, last = (max(0, -steps), min(count, count - steps))
    return lax.ppermute(value, axis, [(source, source + steps) for source in range(initial, last)])


def gelu_grad(values):
    tangent = jnp.tanh(GELU_A * (values + GELU_B * values * values * values))
    return 0.5 * (1.0 + tangent) + 0.5 * values * (1.0 - tangent * tangent) * GELU_A * (
        1.0 + 3.0 * GELU_B * values * values
    )


def mix_bits(flat_index, seed_value, step_value):
    hashed = (
        flat_index * jnp.int32(-1640531535)
        + seed_value * jnp.int32(-2048144777)
        + step_value * jnp.int32(-1028477379)
    )
    hashed = hashed ^ lax.shift_right_logical(hashed, jnp.int32(16))
    hashed = hashed * jnp.int32(2146121005)
    hashed = hashed ^ lax.shift_right_logical(hashed, jnp.int32(15))
    hashed = hashed * jnp.int32(-2073254261)
    hashed = hashed ^ lax.shift_right_logical(hashed, jnp.int32(16))
    return lax.shift_right_logical(hashed, jnp.int32(8)).astype(jnp.float32) / 16777216.0


def tap_windows(series, extra_rows, patches):
    joined = jnp.concatenate([series, extra_rows], 0)
    tail_shape = joined.shape[1:]
    lower = joined[:-STRIDE].reshape((patches, STRIDE) + tail_shape)
    upper = joined[STRIDE:].reshape((patches, STRIDE) + tail_shape)
    return jnp.concatenate([lower, upper], 1)


def per_device(
    byte_rows, cotangent, doc_ids, conv_weight, norm_gain, proj_weight, round_seed, step_count
):
    byte_block = byte_rows[0]
    upstream = cotangent[0]
    doc_block = doc_ids[0]
    length = byte_block.shape[0]
    row_width = byte_block.shape[1]
    patches = length // STRIDE
    panel_rows = proj_weight.shape[0]
    full_width = panel_rows * lax.axis_size("fsdp")
    next_bytes, next_up, next_docs = shifted(
        (byte_block[:STRIDE], upstream[:STRIDE], doc_block[:STRIDE]), "seq", -1
    )
    window = tap_windows(byte_block, next_bytes, patches)
    up_window = tap_windows(upstream, next_up, patches)
    doc_window = tap_windows(doc_block, next_docs, patches)
    is_last = lax.axis_index("seq") == lax.axis_size("seq") - 1
    patch_ids = lax.broadcasted_iota(jnp.int32, (patches, KERNEL), 0)
    tap_ids = lax.broadcasted_iota(jnp.int32, (patches, KERNEL), 1)
    spilled = is_last & (patch_ids == patches - 1) & (tap_ids >= STRIDE)
    keep_tap = (doc_window == doc_window[:, :1]) & jnp.logical_not(spilled)
    keep_f = keep_tap.astype(jnp.float32)[:, :, None]
    masked = window * keep_tap.astype(jnp.bfloat16)[:, :, None]
    grouped = masked.reshape(patches, KERNEL, GROUPS, CG)
    hidden = jnp.einsum(
        "pkgc,kgcd->pgd", grouped, conv_weight, preferred_element_type=jnp.float32
    ).reshape(patches, row_width)
    factor = lax.rsqrt(jnp.mean(hidden * hidden, axis=-1, keepdims=True) + 1e-06)
    normed = (hidden * factor * norm_gain).astype(jnp.bfloat16)
    contract_last = (((1,), (1,)), ((), ()))
    full_proj = lax.all_gather(proj_weight, "fsdp", axis=0, tiled=True)
    pre_act = lax.dot_general(normed, full_proj, contract_last, preferred_element_type=jnp.float32)
    grad_pre = (
        up_window.astype(jnp.float32)
        * keep_f
        * gelu_grad(pre_act.reshape(patches, KERNEL, row_width))
    )
    grad_pre = grad_pre.reshape(patches, full_width).astype(jnp.bfloat16)
    grad_norm = jnp.dot(grad_pre, full_proj, preferred_element_type=jnp.float32)
    contract_first = (((0,), (0,)), ((), ()))
    panel_part = lax.psum_scatter(
        lax.dot_general(grad_pre, normed, contract_first, preferred_element_type=jnp.float32),
        "fsdp",
        scatter_dimension=0,
        tiled=True,
    )
    proj_sum = lax.psum(panel_part, "seq")
    gain_part = jnp.sum(grad_norm * hidden * factor, axis=0)
    gained = norm_gain * grad_norm
    grad_hidden = factor * gained - hidden * factor * factor * factor * jnp.mean(
        gained * hidden, axis=-1, keepdims=True
    )
    grad_hidden = grad_hidden.reshape(patches, GROUPS, CG)
    grouped_f = grouped.astype(jnp.float32)
    conv_f = conv_weight.astype(jnp.float32)
    conv_part = jnp.einsum(
        "pkgc,pgd->kgcd", grouped_f, grad_hidden, precision=lax.Precision.HIGHEST
    )
    gain_sum, conv_sum = lax.psum((gain_part, conv_part), ("seq", "fsdp"))
    grad_window = jnp.einsum("pgd,kgcd->pkgc", grad_hidden, conv_f, precision=lax.Precision.HIGHEST)
    grad_window = grad_window.reshape(patches, KERNEL, row_width) * keep_f
    back_lower = grad_window[:, :STRIDE].reshape(length, row_width)
    back_upper = grad_window[:, STRIDE:].reshape(length, row_width)
    incoming = shifted(back_upper[length - STRIDE :], "seq", 1)
    back_rows = back_lower + jnp.concatenate([incoming, back_upper[: length - STRIDE]], 0)
    grad_bytes = (upstream.astype(jnp.float32) + back_rows)[None]
    total_patches = patches * lax.axis_size("seq") * lax.axis_size("fsdp")
    grad_scale = 1.0 / math.sqrt(total_patches)
    first_panel = lax.axis_index("fsdp") * jnp.int32(panel_rows)
    row_index = first_panel + jnp.arange(panel_rows, dtype=jnp.int32)
    flat_index = (
        row_index[:, None] * jnp.int32(row_width) + jnp.arange(row_width, dtype=jnp.int32)[None, :]
    )
    dither_noise = mix_bits(flat_index, round_seed[0], step_count[0])
    grad_proj = proj_sum * grad_scale + QUANT * (dither_noise - 0.5)
    return (grad_bytes, grad_proj, conv_sum * grad_scale, gain_sum * grad_scale)


def solution(mesh):
    in_specs = (
        P("fsdp", "seq", None),
        P("fsdp", "seq", None),
        P("fsdp", "seq"),
        P(),
        P(),
        P("fsdp", None),
        P(),
        P(),
    )
    out_specs = (P("fsdp", "seq", None), P("fsdp", None), P(), P())
    return jax.shard_map(
        per_device, mesh=mesh, in_specs=in_specs, out_specs=out_specs, check_vma=False
    )
```

profile of v0, /device:TPU:32, one launch (start us, length us, event | category | flops | bytes accessed | tf_op | source)
XLA Modules:
  0.0 572.1 jit_solution(2157465076530851833)
XLA Ops:
  13.9 9.7 %concatenate.46 = bf16[256,4,32,16]{3,2,1,0:T(8,128)(2,1)} reshape(bf16[1,1024,512]{2,1,0:T(8,128)(2,1)} %param.8) | data formatting | bytes 2097152 | tf_op jit(solution)/shard_map/concatenate | solution.py:48
  25.2 9.8 %copy.43 = bf16[256,4,32,16]{0,3,2,1:T(8,128)(2,1)} copy(bf16[256,4,32,16]{3,2,1,0:T(8,128)(2,1)} %concatenate.46) | data formatting | bytes 2097152 | tf_op jit(solution)/shard_map/concatenate | solution.py:48
  35.0 3.1 copy.65
  40.2 8.2 %concatenate.48 = bf16[256,4,32,16]{3,2,1,0:T(8,128)(2,1)} reshape(bf16[1024,512]{1,0:T(8,128)(2,1)S(1)} %pad_maximum_fusion.1) | data formatting | bytes 2097152 | tf_op jit(solution)/shard_map/concatenate | solution.py:48
  48.4 9.8 %copy.44 = bf16[256,4,32,16]{0,3,2,1:T(8,128)(2,1)} copy(bf16[256,4,32,16]{3,2,1,0:T(8,128)(2,1)} %concatenate.48) | data formatting | bytes 2097152 | tf_op jit(solution)/shard_map/concatenate | solution.py:48
  63.6 7.9 %fusion.6 = bf16[256,8,512]{2,0,1:T(8,128)(2,1)} fusion(bf16[256,512,1]{0,1,2:T(8,128)(2,1)S(1)} %bitcast.62, bf16[8,512,512]{2,1,0:T(8,128)(2,1)} %bitcast.67, bf16[256,4,512]{2,0,1:T(8,128)(2,1)} %copy.50, bf16[256,4,512]{2,0,1:T(8,128)(2,1)} %copy.49, f32[256,8]{0,1:T(8,128)S(1)} %get-tuple-element.18), kind=kOutput, calls=%fused_computation.8 | convolution fusion | flops 1096810496 | bytes 8658944 | tf_op jit(solution)/shard_map/dot_general | solution.py:83
  71.5 3.9 copy.52
  75.4 6.1 %fusion.27 = f32[4096,512]{1,0:T(8,128)} fusion(bf16[256,4096]{0,1:T(8,128)(2,1)} %bitcast.55, bf16[256,512]{0,1:T(8,128)(2,1)S(1)} %bitcast.63), kind=kOutput, calls=%fused_computation.54 | convolution fusion | flops 1073741824 | bytes 10747904 | tf_op jit(solution)/shard_map/dot_general | solution.py:93
  81.8 3.5 copy.56
  88.7 4.3 multiply_reduce_fusion
  96.1 3.2 convolution_bitcast_fusion
  99.2 2.6 copy.57
  101.8 5.4 copy.58
  107.2 2.6 broadcast_multiply_fusion
  111.8 5.8 %collective-permute-start.3 = (f32[4,512]{1,0:T(4,128)S(1)}, f32[4,512]{1,0:T(4,128)S(1)}, u32[]{:S(2)}, u32[]{:S(2)}) collective-permute-start(f32[4,512]{1,0:T(4,128)S(1)} %bitcast.65), channel_id=1, source_target_pairs={{0,16},{16,32},{32,48},{48,64},{64,80},{80,96},{96,112},{112,128},... | collective-permute-start | bytes 24584 | tf_op jit(solution)/shard_map/ppermute | solution.py:19
  117.6 82.1 %psum.23 = f32[512]{0:T(512)S(1)} all-reduce(f32[512]{0:T(512)S(1)} %get-tuple-element.16), channel_id=1, replica_groups=mesh['seq'=16,'fsdp'=16] {'seq','fsdp'}, use_global_device_ids=true, to_apply=%region_6.0 | all-reduce | flops 512 | bytes 4096 | tf_op jit(solution)/shard_map/psum | solution.py:110
  199.7 9.8 %fusion.10 = f32[8,32,16,16]{2,3,0,1:T(8,128)} fusion(f32[256,32,16,1]{0,2,3,1:T(8,128)} %bitcast.60, bf16[256,8,32,16]{0,3,2,1:T(8,128)(2,1)S(1)} %maximum_multiply_fusion), kind=kOutput, calls=%fused_computation.16 | convolution fusion | flops 201326592 | bytes 2883584 | tf_op jit(solution)/shard_map/pkgc,pgd->kgcd/dot_general | solution.py:107
  214.2 2.7 copy.59
  216.8 2.9 reshape.243
  219.8 2.7 copy.60
  222.4 3.1 concatenate.56
  225.6 3.5 fusion.7
  229.1 234.9 %all-reduce.5.cloned.1.call-done = f32[8,32,16,16]{2,3,0,1:T(8,128)} async-done(((f32[8,32,16,16]{2,3,0,1:T(8,128)}), f32[8,32,16,16]{2,3,0,1:T(8,128)}) %all-reduce.5.cloned.1.call-update) | async-done | bytes 262160 | tf_op jit(solution)/shard_map/psum | solution.py:110
  468.1 95.2 %all-reduce.3.cloned.1.call-done = f32[256,512]{1,0:T(8,128)} async-done(((f32[256,512]{1,0:T(8,128)}), f32[256,512]{1,0:T(8,128)}) %all-reduce.3.cloned.1.call-update) | async-done | bytes 524304 | tf_op jit(solution)/shard_map/psum | solution.py:98
  (81 shorter events, 33.9 us)
Async XLA Ops:
  7.2 56.5 %all-gather.2.cloned.1.call-start = ((), (), s32[]{:S(2)}) async-start(), calls=%async_computation.1 | async-start | bytes 4456448 | tf_op jit(solution)/shard_map/all_gather | solution.py:82
  7.9 217.7 %reduce-scatter.2.cloned.1.call-start = ((), (), s32[]{:S(2)}) async-start(), calls=%async_computation.2 | async-start | bytes 8912896 | tf_op jit(solution)/shard_map/reduce_scatter | solution.py:92
  8.6 30.9 %collective-permute-start.1 = (s32[4]{0:T(128)S(1)}, s32[4]{0:T(128)S(1)}, u32[]{:S(2)}, u32[]{:S(2)}) collective-permute-start(s32[4]{0:T(128)S(1)} %slice_bitcast_fusion.2), channel_id=1, source_target_pairs={{16,0},{32,16},{48,32},{64,48},{80,64},{96,80},{112,96},{128,112},... | collective-permute-start | bytes 56 | tf_op jit(solution)/shard_map/ppermute | solution.py:19
  10.6 29.3 %collective-permute-start = (bf16[4,512]{1,0:T(4,128)(2,1)S(1)}, bf16[4,512]{1,0:T(4,128)(2,1)S(1)}, u32[]{:S(2)}, u32[]{:S(2)}) collective-permute-start(bf16[4,512]{1,0:T(4,128)(2,1)S(1)} %slice_bitcast_fusion.1), channel_id=1, source_target_pairs={{16,0},{32,16},{48,32},{64,48},{80,64},{96,80},{112,96},{128,112},... | collective-permute-start | bytes 12296 | tf_op jit(solution)/shard_map/ppermute | solution.py:19
  12.6 45.6 %collective-permute-start.2 = (bf16[4,512]{1,0:T(4,128)(2,1)S(1)}, bf16[4,512]{1,0:T(4,128)(2,1)S(1)}, u32[]{:S(2)}, u32[]{:S(2)}) collective-permute-start(bf16[4,512]{1,0:T(4,128)(2,1)S(1)} %slice_bitcast_fusion), channel_id=1, source_target_pairs={{16,0},{32,16},{48,32},{64,48},{80,64},{96,80},{112,96},{128,112},... | collective-permute-start | bytes 12296 | tf_op jit(solution)/shard_map/ppermute | solution.py:19
  13.9 9.7 %copy-start.2 = (bf16[1,1024,512]{2,1,0:T(8,128)(2,1)S(1)}, bf16[1,1024,512]{2,1,0:T(8,128)(2,1)}, u32[]{:S(2)}) copy-start(bf16[1,1024,512]{2,1,0:T(8,128)(2,1)} %param.9) | copy-start | bytes 3145732
  23.6 0.8 copy-start.10
  25.2 12.9 %copy-start.11 = (f32[512]{0:T(512)S(1)}, f32[512]{0:T(512)}, u32[]{:S(2)}) copy-start(f32[512]{0:T(512)} %param.12) | copy-start | bytes 6148
  35.0 4.9 copy-start.5
  58.8 1.4 copy-start.6
  58.8 1.9 copy-start.7
  60.7 1.2 copy-start.8
  62.7 0.8 copy-start.4
  81.6 382.5 %all-reduce.5.cloned.1.call-start = ((), (), s32[]{:S(2)}) async-start(), calls=%async_computation.4 | async-start | bytes 4194304 | tf_op jit(solution)/shard_map/psum | solution.py:110
  88.7 4.4 copy-start.9
  109.8 2.0 copy-start
  111.8 113.8 %collective-permute-start.3 = (f32[4,512]{1,0:T(4,128)S(1)}, f32[4,512]{1,0:T(4,128)S(1)}, u32[]{:S(2)}, u32[]{:S(2)}) collective-permute-start(f32[4,512]{1,0:T(4,128)S(1)} %bitcast.65), channel_id=1, source_target_pairs={{0,16},{16,32},{32,48},{48,64},{64,80},{80,96},{96,112},{112,128},... | collective-permute-start | bytes 24584 | tf_op jit(solution)/shard_map/ppermute | solution.py:19
  209.5 353.8 %all-reduce.3.cloned.1.call-start = ((), (), s32[]{:S(2)}) async-start(), calls=%async_computation.3 | async-start | bytes 1048576 | tf_op jit(solution)/shard_map/psum | solution.py:98
  210.4 2.2 copy-start.1
  212.6 1.6 slice-start
  222.4 3.2 copy-start.3
Sparse Core Ops, SparseCore 0:
  9.8 44.4 all-gather.1
  81.7 75.4 reduce-scatter.1
  209.6 254.3 all-reduce.4
  467.1 96.1 all-reduce.2
where the time goes:
time: 574 us; the launch traced here: 572 us
  waiting for transfers between devices  331 us (58%)
  local copies, waits for them, and re-layouts  88.1 us (15%)
  blocking collectives  82.1 us (14%)
  matrix products  32.1 us (6%)
  between operations  15.3 us (3%)
  other arithmetic  13.3 us (2%)
  starting transfers between devices  10.2 us (2%)
    psum x1, waiting for transfers between devices, per_device(): gain_sum, conv_sum = lax.psum((gain_part, conv_part), ('seq', 'fsdp'))  235 us
    psum x1, waiting for transfers between devices, per_device(): proj_sum = lax.psum(panel_part, 'seq')  95.2 us
    psum x1, blocking collectives, per_device(): gain_sum, conv_sum = lax.psum((gain_part, conv_part), ('seq', 'fsdp'))  82.1 us
    concatenate x6, local copies, waits for them, and re-layouts, tap_windows(): return jnp.concatenate([lower, upper], 1)  37.7 us
    unnamed x29, local copies, waits for them, and re-layouts  16.2 us
  transfers between devices with their start and end apart: 8, of which 2 were waited for; matrix products, arithmetic and copies ran while one was open for 18% of the time, Pallas kernels for 0%

commit v1 on v0

--- a/solution.py
+++ b/solution.py
@@ -11,6 +11,11 @@
 GELU_A = 0.7978845608028654
 GELU_B = 0.044715
 QUANT = 0.25
+
+
+def one_after_other(value_2, one, other):
+    partial = lax.psum(value_2, one)
+    return lax.psum(partial, other)
 
 
 def shifted(value, axis, steps):
@@ -107,7 +112,7 @@
     conv_part = jnp.einsum(
         "pkgc,pgd->kgcd", grouped_f, grad_hidden, precision=lax.Precision.HIGHEST
     )
-    gain_sum, conv_sum = lax.psum((gain_part, conv_part), ("seq", "fsdp"))
+    gain_sum, conv_sum = one_after_other((gain_part, conv_part), "fsdp", "seq")
     grad_window = jnp.einsum("pgd,kgcd->pkgc", grad_hidden, conv_f, precision=lax.Precision.HIGHEST)
     grad_window = grad_window.reshape(patches, KERNEL, row_width) * keep_f
     back_lower = grad_window[:, :STRIDE].reshape(length, row_width)

time: 574 us -> 412 us (0.72)
  waiting for transfers between devices: 331 us -> 192 us
  blocking collectives: 82.1 us -> 63.8 us
    psum x1, waiting for transfers between devices: 235 us -> 101 us  [one_after_other(): partial = lax.psum(value_2, one)]
    psum x1, waiting for transfers between devices: 95.2 us -> 18 us  [per_device(): proj_sum = lax.psum(panel_part, 'seq')]
    reduce_scatter x1, waiting for transfers between devices: 0.01 us -> 72.6 us  [per_device(): lax.psum_scatter(lax.dot_general(grad_pre, normed, contract_first, prefer...]
    psum x1 -> x2, blocking collectives: 82.1 us -> 63.8 us  [the longest x1 38.5 us: one_after_other(): return lax.psum(partial, other)]
    unnamed x29 -> x35, local copies, waits for them, and re-layouts: 16.2 us -> 16.1 us
  transfers between devices with their start and end apart: 8 -> 8, of which waited for: 2 -> 3; matrix products, arithmetic and copies ran while one was open for 18% -> 21% of each run, Pallas kernels for 0% -> 0%
where the time goes in v1:
time: 412 us; the launch traced here: 410 us
  waiting for transfers between devices  192 us (47%)
  local copies, waits for them, and re-layouts  88.1 us (21%)
  blocking collectives  63.8 us (15%)
  matrix products  29.9 us (7%)
  between operations  15.3 us (4%)
  other arithmetic  13.2 us (3%)
  starting transfers between devices  7.45 us (2%)
    psum x1, waiting for transfers between devices, one_after_other(): partial = lax.psum(value_2, one)  101 us
    reduce_scatter x1, waiting for transfers between devices, per_device(): lax.psum_scatter(lax.dot_general(grad_pre, normed, contract_first, prefer...  72.6 us
    psum x1, blocking collectives, one_after_other(): return lax.psum(partial, other)  38.5 us
    concatenate x6, local copies, waits for them, and re-layouts, tap_windows(): return jnp.concatenate([lower, upper], 1)  37.7 us
    psum x1, blocking collectives, one_after_other(): partial = lax.psum(value_2, one)  25.2 us
    psum x1, waiting for transfers between devices, per_device(): proj_sum = lax.psum(panel_part, 'seq')  18 us
    unnamed x35, local copies, waits for them, and re-layouts  16.1 us
    dot_general x1, matrix products, per_device(): jnp.einsum('pkgc,pgd->kgcd', grouped_f, grad_hidden, precision=lax.Precis...  9.77 us
  transfers between devices with their start and end apart: 8, of which 3 were waited for; matrix products, arithmetic and copies ran while one was open for 21% of the time, Pallas kernels for 0%

profile of v1, /device:TPU:32, one launch (start us, length us, event | category | flops | bytes accessed | tf_op | source)
XLA Modules:
  0.0 409.6 jit_solution(15400910056296855744)
XLA Ops:
  13.9 9.7 %concatenate.46 = bf16[256,4,32,16]{3,2,1,0:T(8,128)(2,1)} reshape(bf16[1,1024,512]{2,1,0:T(8,128)(2,1)} %param.8) | data formatting | bytes 2097152 | tf_op jit(solution)/shard_map/concatenate | solution.py:53
  25.3 9.8 %copy.43 = bf16[256,4,32,16]{0,3,2,1:T(8,128)(2,1)} copy(bf16[256,4,32,16]{3,2,1,0:T(8,128)(2,1)} %concatenate.46) | data formatting | bytes 2097152 | tf_op jit(solution)/shard_map/concatenate | solution.py:53
  35.1 3.1 copy.65
  40.3 8.2 %concatenate.48 = bf16[256,4,32,16]{3,2,1,0:T(8,128)(2,1)} reshape(bf16[1024,512]{1,0:T(8,128)(2,1)S(1)} %pad_maximum_fusion.1) | data formatting | bytes 2097152 | tf_op jit(solution)/shard_map/concatenate | solution.py:53
  48.5 9.8 %copy.44 = bf16[256,4,32,16]{0,3,2,1:T(8,128)(2,1)} copy(bf16[256,4,32,16]{3,2,1,0:T(8,128)(2,1)} %concatenate.48) | data formatting | bytes 2097152 | tf_op jit(solution)/shard_map/concatenate | solution.py:53
  66.8 7.9 %fusion.6 = bf16[256,8,512]{2,0,1:T(8,128)(2,1)} fusion(bf16[256,512,1]{0,1,2:T(8,128)(2,1)S(1)} %bitcast.62, bf16[8,512,512]{2,1,0:T(8,128)(2,1)} %bitcast.67, bf16[256,4,512]{2,0,1:T(8,128)(2,1)} %copy.50, bf16[256,4,512]{2,0,1:T(8,128)(2,1)} %copy.49, f32[256,8]{0,1:T(8,128)S(1)} %get-tuple-element.20), kind=kOutput, calls=%fused_computation.8 | convolution fusion | flops 1096810496 | bytes 8658944 | tf_op jit(solution)/shard_map/dot_general | solution.py:88
  74.7 3.9 copy.52
  78.6 4.3 %multiply_reduce_fusion = (f32[512]{0:T(512)S(1)}, f32[256]{0:T(256)S(1)}, f32[256,512]{1,0:T(8,128)S(1)}) fusion(f32[256,512]{1,0:T(8,128)} %copy.53, f32[256]{0:T(256)S(1)} %add_rsqrt_fusion, f32[512]{0:T(512)S(1)} %copy-done.14, bf16[256,4096]{0,1:T(8,128)(2,1)} %bitcast.55, bf16[4096,512]{1,0:T(8,128)(2,1)} %all-gather.2.cloned.1.call-done), kind=kOutput, calls=%fused_computation.36 | convolution fusion | flops 1074527488 | bytes 7346176 | tf_op jit(solution)/shard_map/dot_general | solution.py:95
  85.9 9.8 %fusion.10 = f32[8,32,16,16]{2,3,0,1:T(8,128)} fusion(f32[256,32,16,1]{0,2,3,1:T(8,128)} %bitcast.59, bf16[256,8,32,16]{0,3,2,1:T(8,128)(2,1)S(1)} %maximum_multiply_fusion), kind=kOutput, calls=%fused_computation.16 | convolution fusion | flops 201326592 | bytes 2883584 | tf_op jit(solution)/shard_map/pkgc,pgd->kgcd/dot_general | solution.py:112
  97.3 4.5 %fusion.27 = f32[4096,512]{1,0:T(8,128)} fusion(bf16[256,4096]{0,1:T(8,128)(2,1)S(1)} %bitcast.56, bf16[256,512]{0,1:T(8,128)(2,1)S(1)} %bitcast.63), kind=kOutput, calls=%fused_computation.54 | convolution fusion | flops 1073741824 | bytes 10747904 | tf_op jit(solution)/shard_map/dot_general | solution.py:98
  107.8 2.6 copy.57
  110.3 5.4 %copy.58 = f32[256,8,512]{2,0,1:T(8,128)} copy(f32[256,8,512]{0,2,1:T(8,128)} %bitcast.54) | data formatting | bytes 8388608 | tf_op jit(solution)/shard_map/reshape | solution.py:117
  115.7 100.5 %all-reduce.4.cloned.1.call-done = f32[8,32,16,16]{2,3,0,1:T(8,128)} async-done(((f32[8,32,16,16]{2,3,0,1:T(8,128)}), f32[8,32,16,16]{2,3,0,1:T(8,128)}) %all-reduce.4.cloned.1.call-update) | async-done | bytes 262160 | tf_op jit(solution)/shard_map/psum | solution.py:17
  216.2 72.6 %reduce-scatter.2.cloned.1.call-done = f32[256,512]{1,0:T(8,128)} async-done(((f32[4096,512]{1,0:T(8,128)}), f32[256,512]{1,0:T(8,128)}) %reduce-scatter.2.cloned.1.call-update) | async-done | bytes 524304 | tf_op jit(solution)/shard_map/reduce_scatter | solution.py:97
  288.8 2.5 broadcast_multiply_fusion
  293.3 3.5 collective-permute-start.3
  296.8 25.2 %psum.38 = f32[512]{0:T(512)S(1)} all-reduce(f32[512]{0:T(512)S(1)} %get-tuple-element.16), channel_id=1, replica_groups=mesh['seq'=16,'fsdp'=16] {'fsdp'}, use_global_device_ids=true, to_apply=%region_7.0 | all-reduce | flops 512 | bytes 4096 | tf_op jit(solution)/shard_map/psum | solution.py:17
  322.0 38.5 %psum.39 = f32[512]{0:T(512)S(1)} all-reduce(f32[512]{0:T(512)S(1)} %psum.38), channel_id=1, replica_groups=mesh['seq'=16,'fsdp'=16] {'seq'}, use_global_device_ids=true, to_apply=%region_8.0 | all-reduce | flops 512 | bytes 4096 | tf_op jit(solution)/shard_map/psum | solution.py:18
  364.9 2.7 copy.59
  367.6 3.0 reshape.243
  370.6 2.7 copy.60
  373.3 3.1 concatenate.56
  376.4 3.5 fusion.7
  379.9 18.0 %all-reduce.6.cloned.1.call-done = (f32[256,512]{1,0:T(8,128)}, f32[8,32,16,16]{2,3,0,1:T(8,128)}) async-done(((f32[256,512]{1,0:T(8,128)}, f32[8,32,16,16]{2,3,0,1:T(8,128)}), (f32[256,512]{1,0:T(8,128)}, f32[8,32,16,16]{2,3,0,1:T(8,128)})) %all-reduce.6.cloned.1.call-update) | async-done | bytes 786448 | tf_op jit(solution)/shard_map/psum | solution.py:103
  (88 shorter events, 39.5 us)
Async XLA Ops:
  7.2 59.6 %all-gather.2.cloned.1.call-start = ((), (), s32[]{:S(2)}) async-start(), calls=%async_computation.1 | async-start | bytes 4456448 | tf_op jit(solution)/shard_map/all_gather | solution.py:87
  7.9 208.3 %all-reduce.4.cloned.1.call-start = ((), (), s32[]{:S(2)}) async-start(), calls=%async_computation.3 | async-start | bytes 4194304 | tf_op jit(solution)/shard_map/psum | solution.py:17
  8.6 31.0 %collective-permute-start.1 = (s32[4]{0:T(128)S(1)}, s32[4]{0:T(128)S(1)}, u32[]{:S(2)}, u32[]{:S(2)}) collective-permute-start(s32[4]{0:T(128)S(1)} %slice_bitcast_fusion.2), channel_id=1, source_target_pairs={{16,0},{32,16},{48,32},{64,48},{80,64},{96,80},{112,96},{128,112},... | collective-permute-start | bytes 56 | tf_op jit(solution)/shard_map/ppermute | solution.py:24
  10.6 29.4 %collective-permute-start = (bf16[4,512]{1,0:T(4,128)(2,1)S(1)}, bf16[4,512]{1,0:T(4,128)(2,1)S(1)}, u32[]{:S(2)}, u32[]{:S(2)}) collective-permute-start(bf16[4,512]{1,0:T(4,128)(2,1)S(1)} %slice_bitcast_fusion.1), channel_id=1, source_target_pairs={{16,0},{32,16},{48,32},{64,48},{80,64},{96,80},{112,96},{128,112},... | collective-permute-start | bytes 12296 | tf_op jit(solution)/shard_map/ppermute | solution.py:24
  12.6 45.7 %collective-permute-start.2 = (bf16[4,512]{1,0:T(4,128)(2,1)S(1)}, bf16[4,512]{1,0:T(4,128)(2,1)S(1)}, u32[]{:S(2)}, u32[]{:S(2)}) collective-permute-start(bf16[4,512]{1,0:T(4,128)(2,1)S(1)} %slice_bitcast_fusion), channel_id=1, source_target_pairs={{16,0},{32,16},{48,32},{64,48},{80,64},{96,80},{112,96},{128,112},... | collective-permute-start | bytes 12296 | tf_op jit(solution)/shard_map/ppermute | solution.py:24
  13.9 9.7 %copy-start.3 = (bf16[1,1024,512]{2,1,0:T(8,128)(2,1)S(1)}, bf16[1,1024,512]{2,1,0:T(8,128)(2,1)}, u32[]{:S(2)}) copy-start(bf16[1,1024,512]{2,1,0:T(8,128)(2,1)} %param.9) | copy-start | bytes 3145732
  23.6 0.8 copy-start.13
  25.3 12.9 %copy-start.14 = (f32[512]{0:T(512)S(1)}, f32[512]{0:T(512)}, u32[]{:S(2)}) copy-start(f32[512]{0:T(512)} %param.12) | copy-start | bytes 6148
  35.1 4.9 %copy-start.6 = (bf16[1,1024,512]{2,1,0:T(8,128)(2,1)S(1)}, bf16[1,1024,512]{2,1,0:T(8,128)(2,1)}, u32[]{:S(2)}) copy-start(bf16[1,1024,512]{2,1,0:T(8,128)(2,1)} %param.8) | copy-start | bytes 3145732
  58.8 1.4 copy-start.7
  58.8 1.9 copy-start.8
  60.7 1.2 copy-start.9
  78.6 4.4 %copy-start.11 = (f32[256,512]{1,0:T(8,128)S(1)}, f32[256,512]{1,0:T(8,128)}, u32[]{:S(2)}) copy-start(f32[256,512]{1,0:T(8,128)} %copy.53) | copy-start | bytes 1572868
  95.7 1.6 copy-start.2
  95.7 193.1 %reduce-scatter.2.cloned.1.call-start = ((), (), s32[]{:S(2)}) async-start(), calls=%async_computation.2 | async-start | bytes 8912896 | tf_op jit(solution)/shard_map/reduce_scatter | solution.py:97
  101.8 1.0 copy-start.10
  101.8 4.1 %copy-start.5 = (f32[256,512]{0,1:T(8,128)S(1)}, f32[256,512]{0,1:T(8,128)}, u32[]{:S(2)}) copy-start(f32[256,512]{0,1:T(8,128)} %copy.55) | copy-start | bytes 1572868
  101.9 296.0 %all-reduce.6.cloned.1.call-start = ((), (), s32[]{:S(2)}) async-start(), calls=%async_computation.4 | async-start | bytes 5242880 | tf_op jit(solution)/shard_map/psum | solution.py:103
  291.4 1.9 copy-start
  293.3 83.0 %collective-permute-start.3 = (f32[4,512]{1,0:T(4,128)S(1)}, f32[4,512]{1,0:T(4,128)S(1)}, u32[]{:S(2)}, u32[]{:S(2)}) collective-permute-start(f32[4,512]{1,0:T(4,128)S(1)} %bitcast.65), channel_id=1, source_target_pairs={{0,16},{16,32},{32,48},{48,64},{64,80},{80,96},{96,112},{112,128},... | collective-permute-start | bytes 24584 | tf_op jit(solution)/shard_map/ppermute | solution.py:24
  361.1 2.2 copy-start.1
  363.4 1.6 slice-start
  373.3 3.1 copy-start.4
  399.6 2.3 copy-start.12
Sparse Core Ops, SparseCore 0:
  9.8 44.4 all-gather.1
  95.9 120.3 all-reduce.3
  218.8 69.9 reduce-scatter.1
  292.1 105.6 all-reduce.5
